TPU v7x, 256 devices: a whole 4x4x8 slice. The times are simulated.
256 devices in a mesh: ent: 64 (over z, y, core), rep: 4 (over x).
Axes of the slice: x: 4, y: 4, z: 8, core: 2. Of those that a mesh axis runs over, the one named last changes fastest.
Arguments:
- table: float32 [262144, 256], P('ent'), may hold values from -6.1 to 6.1
- relations: float32 [824, 256], P('rep'), may hold values from -4 to 4
- anchor: int32 [2048], P('rep'), may hold values from 0 to 262143
- rel_one: int32 [2048], P('rep'), may hold values from 0 to 823
- rel_two: int32 [2048], P('rep'), may hold values from 0 to 823
Outputs:
- log_answer: float32 [2048, 262144], P('rep', 'ent')
All inputs are finite; a program needn't handle non-finite values.
Results may differ from a plain program's by a relative error of at most 0.00018.
Values sent between devices are 32-bit elements; how exact they have to be, the bound alone decides.
No kernel may reach another device: no remote copies, remote signals or barrier semaphores. Data moves between devices by JAX's collectives and lax.ppermute only.
A program may use at most 128 MiB of HBM per device.

v0:
```python
import jax
import jax.numpy as jnp
from jax import lax
from jax.sharding import PartitionSpec as P


def cmul(left, right):
    half = left.shape[1] // 2
    lre, lim = (left[:, :half], left[:, half:])
    rre, rim = (right[:, :half], right[:, half:])
    return jnp.concatenate([lre * rre - lim * rim, lre * rim + lim * rre], axis=1)


def against(query, table):
    return lax.dot_general(
        query,
        table,
        (((1,), (1,)), ((), ())),
        precision=lax.Precision.HIGHEST,
        preferred_element_type=jnp.float32,
    )


def weighted(weights, table):
    return jnp.dot(
        weights, table, precision=lax.Precision.HIGHEST, preferred_element_type=jnp.float32
    )


def on_device(table, relations, anchor, rel_one, rel_two):
    rows = table.shape[0]
    start = lax.axis_index("ent") * rows
    offset = anchor - start
    inside = ((offset >= 0) & (offset < rows)).astype(jnp.float32)
    local_rows = jnp.take(table, jnp.clip(offset, 0, rows - 1), axis=0)
    anchor_emb = lax.psum(local_rows * inside[:, None], "ent")
    rel_all = lax.all_gather(relations, "rep", axis=0, tiled=True)
    rel_first = jnp.take(rel_all, rel_one, axis=0)
    rel_second = jnp.take(rel_all, rel_two, axis=0)
    query_one = cmul(anchor_emb, rel_first)
    scores = against(query_one, table)
    local_peak = jnp.max(scores, axis=1)
    peak = lax.pmax(local_peak, "ent")
    weights = jnp.exp(scores - peak[:, None])
    total, summed = lax.psum((jnp.sum(weights, axis=1), weighted(weights, table)), "ent")
    query_two = cmul(summed / total[:, None], rel_second)
    scores_two = against(query_two, table)
    local_top = jnp.max(scores_two, axis=1)
    top = lax.pmax(local_top, "ent")
    shifted = scores_two - top[:, None]
    mass = lax.psum(jnp.sum(jnp.exp(shifted), axis=1), "ent")
    return shifted - jnp.log(mass)[:, None]


def solution(mesh):
    in_specs = (P("ent", None), P("rep", None), P("rep"), P("rep"), P("rep"))
    out_specs = P("rep", "ent")
    return jax.shard_map(
        on_device, mesh=mesh, in_specs=in_specs, out_specs=out_specs, check_vma=False
    )
```

profile of v0, /device:TPU:1, one launch (start us, length us, event | category | flops | bytes accessed | tf_op | source)
XLA Modules:
  0.0 810.7 jit_solution(4289145787885844124)
XLA Ops:
  6.5 0.0 all-reduce.3.cloned.1.call-start
  6.5 0.7 compare_and_fusion.2
  7.2 3.8 gather_fusion
  11.0 1.0 select_multiply_fusion
  12.0 0.0 all-reduce.3.cloned.1.call-update
  12.0 0.0 all-reduce.5.cloned.1.call-start
  12.1 0.7 compare_and_fusion.1
  12.8 0.7 compare_select_fusion.1
  13.4 0.7 compare_and_fusion
  14.1 0.7 compare_select_fusion
  14.8 13.3 %all-gather = f32[4,206,256]{2,1,0:T(8,128)S(1)} all-gather(f32[1,206,256]{2,1,0:T(8,128)} %bitcast.4), channel_id=1, replica_groups=mesh['ent'=64,'rep'=4] {'rep'}, dimensions={0}, use_global_device_ids=true | all-gather | bytes 1054720 | tf_op jit(solution)/shard_map/all_gather | solution.py:37
  28.1 0.1 reshape.43
  28.2 1.6 gather_fusion.1
  29.8 0.1 broadcast_select_fusion.1
  30.0 1.6 gather_fusion.2
  31.5 0.1 broadcast_select_fusion
  31.7 165.3 %all-reduce.3.cloned.1.call-done = f32[512,256]{1,0:T(8,128)} async-done(((f32[512,256]{1,0:T(8,128)}), f32[512,256]{1,0:T(8,128)}) %all-reduce.3.cloned.1.call-update) | async-done | bytes 524304 | tf_op jit(solution)/shard_map/psum | solution.py:36
  197.0 1.1 multiply_subtract_fusion.1
  198.1 10.9 %fusion.13 = (f32[512]{0:T(512)S(1)}, f32[512,4096]{1,0:T(8,128)}) fusion(f32[4096,256]{1,0:T(8,128)} %param.7, f32[512,128]{1,0:T(8,128)S(1)} %get-tuple-element.11, f32[512,128]{1,0:T(8,128)S(1)} %get-tuple-element.10), kind=kOutput, calls=%fused_computation.37 | convolution fusion | flops 6444678656 | bytes 13109248 | tf_op jit(solution)/shard_map/dot_general | solution.py:15
  209.0 126.3 %pmax.14 = f32[512]{0:T(512)S(1)} all-reduce(f32[512]{0:T(512)S(1)} %get-tuple-element.13), channel_id=1, replica_groups=mesh['ent'=64,'rep'=4] {'ent'}, use_global_device_ids=true, to_apply=%region_2.4 | all-reduce | flops 512 | bytes 4096 | tf_op jit(solution)/shard_map/pmax | solution.py:43
  335.3 11.2 %fusion.1 = f32[512,256]{1,0:T(8,128)} fusion(f32[4096,256]{1,0:T(8,128)} %param.7, f32[512,4096]{1,0:T(8,128)} %get-tuple-element.14, f32[512]{0:T(512)S(1)} %pmax.14), kind=kOutput, calls=%fused_computation.7 | convolution fusion | flops 6444548096 | bytes 13109248 | tf_op jit(solution)/shard_map/dot_general | solution.py:25
  346.5 0.0 all-reduce.5.cloned.1.call-update
  346.5 4.6 fusion
  351.1 125.4 %psum.30 = f32[512]{0:T(512)S(1)} all-reduce(f32[512]{0:T(512)S(1)} %fusion), channel_id=1, replica_groups=mesh['ent'=64,'rep'=4] {'ent'}, use_global_device_ids=true, to_apply=%region_5.7 | all-reduce | flops 512 | bytes 4096 | tf_op jit(solution)/shard_map/psum | solution.py:45
  476.5 50.5 %all-reduce.5.cloned.1.call-done = f32[512,256]{1,0:T(8,128)} async-done(((f32[512,256]{1,0:T(8,128)}), f32[512,256]{1,0:T(8,128)}) %all-reduce.5.cloned.1.call-update) | async-done | bytes 524304 | tf_op jit(solution)/shard_map/psum | solution.py:45
  527.0 1.2 broadcast_divide_fusion
  528.2 0.1 multiply_subtract_fusion
  528.3 10.9 %fusion.14 = (f32[512]{0:T(512)S(1)}, f32[512,4096]{1,0:T(8,128)}) fusion(f32[4096,256]{1,0:T(8,128)} %param.7, f32[512,128]{1,0:T(8,128)S(1)} %get-tuple-element.9, f32[512,128]{1,0:T(8,128)S(1)} %get-tuple-element.8), kind=kOutput, calls=%fused_computation.38 | convolution fusion | flops 6444678656 | bytes 13109248 | tf_op jit(solution)/shard_map/dot_general | solution.py:15
  539.2 126.3 %pmax.15 = f32[512]{0:T(512)S(1)} all-reduce(f32[512]{0:T(512)S(1)} %get-tuple-element.15), channel_id=1, replica_groups=mesh['ent'=64,'rep'=4] {'ent'}, use_global_device_ids=true, to_apply=%region_7.9 | all-reduce | flops 512 | bytes 4096 | tf_op jit(solution)/shard_map/pmax | solution.py:49
  665.5 4.6 exponential_reduce_fusion
  670.1 125.2 %psum.31 = f32[512]{0:T(512)S(1)} all-reduce(f32[512]{0:T(512)S(1)} %exponential_reduce_fusion), channel_id=1, replica_groups=mesh['ent'=64,'rep'=4] {'ent'}, use_global_device_ids=true, to_apply=%region_9.11 | all-reduce | flops 512 | bytes 4096 | tf_op jit(solution)/shard_map/psum | solution.py:51
  795.3 8.6 %subtract_subtract_fusion = f32[512,4096]{1,0:T(8,128)} fusion(f32[512,4096]{1,0:T(8,128)} %get-tuple-element.16, f32[512]{0:T(512)S(1)} %log.3, f32[512]{0:T(512)S(1)} %pmax.15), kind=kLoop, calls=%fused_computation.5 | loop fusion | flops 4194304 | bytes 16781312 | tf_op jit(solution)/shard_map/sub | solution.py:52
  (4 shorter events, 0.0 us)
Async XLA Ops:
  6.5 190.5 %all-reduce.3.cloned.1.call-start = ((), (), s32[]{:S(2)}) async-start(), calls=%async_computation | async-start | bytes 1048576 | tf_op jit(solution)/shard_map/psum | solution.py:36
  12.0 515.0 %all-reduce.5.cloned.1.call-start = ((), (), s32[]{:S(2)}) async-start(), calls=%async_computation.1 | async-start | bytes 1048576 | tf_op jit(solution)/shard_map/psum | solution.py:45
Sparse Core Ops, SparseCore 0:
  12.1 184.8 all-reduce.2
  346.6 180.3 all-reduce.4
where the time goes:
time: 811 us
  blocking collectives  516 us (64%)
  waiting for transfers between devices  216 us (27%)
  matrix products  33 us (4%)
  other arithmetic  24.9 us (3%)
  between operations  13.5 us (2%)
    psum x1, waiting for transfers between devices, on_device(): anchor_emb = lax.psum(local_rows * inside[:, None], 'ent')  165 us
    pmax x1, blocking collectives, on_device(): peak = lax.pmax(local_peak, 'ent')  126 us
    pmax x1, blocking collectives, on_device(): top = lax.pmax(local_top, 'ent')  126 us
    psum x1, blocking collectives, on_device(): lax.psum((jnp.sum(weights, axis=1), weighted(weights, table)), 'ent')  125 us
    psum x1, blocking collectives, on_device(): mass = lax.psum(jnp.sum(jnp.exp(shifted), axis=1), 'ent')  125 us
    psum x1, waiting for transfers between devices, on_device(): lax.psum((jnp.sum(weights, axis=1), weighted(weights, table)), 'ent')  50.5 us
    dot_general x2, matrix products, against(): lax.dot_general(query, table, (((1,), (1,)), ((), ())), precision=lax.Pre...  21.8 us
  transfers between devices with their start and end apart: 2, of which 2 were waited for; matrix products, arithmetic and copies ran while one was open for 1% of the time, Pallas kernels for 0%

commit v1 on v0

--- a/solution.py
+++ b/solution.py
@@ -48,7 +48,7 @@
     local_top = jnp.max(scores_two, axis=1)
     top = lax.pmax(local_top, "ent")
     shifted = scores_two - top[:, None]
-    mass = lax.psum(jnp.sum(jnp.exp(shifted), axis=1), "ent")
+    mass = jnp.sum(lax.all_gather(jnp.sum(jnp.exp(shifted), axis=1), "ent"), axis=0)
     return shifted - jnp.log(mass)[:, None]
 
 

time: 811 us -> 735 us (0.906)
  blocking collectives: 516 us -> 439 us
    psum x1 -> x0, blocking collectives: 125 us -> none  [on_device(): mass = lax.psum(jnp.sum(jnp.exp(shifted), axis=1), 'ent')]
    all_gather x0 -> x1, blocking collectives: none -> 48.2 us  [on_device(): lax.all_gather(jnp.sum(jnp.exp(shifted), axis=1), 'ent')]
where the time goes in v1:
time: 735 us; the launch traced here: 734 us
  blocking collectives  439 us (60%)
  waiting for transfers between devices  216 us (29%)
  matrix products  33 us (4%)
  other arithmetic  25 us (3%)
  between operations  13.5 us (2%)
    psum x1, waiting for transfers between devices, on_device(): anchor_emb = lax.psum(local_rows * inside[:, None], 'ent')  165 us
    pmax x1, blocking collectives, on_device(): peak = lax.pmax(local_peak, 'ent')  126 us
    pmax x1, blocking collectives, on_device(): top = lax.pmax(local_top, 'ent')  126 us
    psum x1, blocking collectives, on_device(): lax.psum((jnp.sum(weights, axis=1), weighted(weights, table)), 'ent')  125 us
    psum x1, waiting for transfers between devices, on_device(): lax.psum((jnp.sum(weights, axis=1), weighted(weights, table)), 'ent')  50.5 us
    all_gather x1, blocking collectives, on_device(): lax.all_gather(jnp.sum(jnp.exp(shifted), axis=1), 'ent')  48.2 us
    dot_general x2, matrix products, against(): lax.dot_general(query, table, (((1,), (1,)), ((), ())), precision=lax.Pre...  21.8 us
  transfers between devices with their start and end apart: 2, of which 2 were waited for; matrix products, arithmetic and copies ran while one was open for 1% of the time, Pallas kernels for 0%

profile of v1, /device:TPU:1, one launch (start us, length us, event | category | flops | bytes accessed | tf_op | source)
XLA Modules:
  0.0 733.9 jit_solution(2550703486523544713)
XLA Ops:
  6.5 0.0 all-reduce.3.cloned.1.call-start
  6.5 0.7 compare_and_fusion.2
  7.2 3.8 gather_fusion
  11.0 1.0 select_multiply_fusion
  12.0 0.0 all-reduce.3.cloned.1.call-update
  12.0 0.0 all-reduce.5.cloned.1.call-start
  12.1 0.7 compare_and_fusion.1
  12.8 0.7 compare_select_fusion.1
  13.4 0.7 compare_and_fusion
  14.1 0.7 compare_select_fusion
  14.8 13.3 %all-gather.1 = f32[4,206,256]{2,1,0:T(8,128)S(1)} all-gather(f32[1,206,256]{2,1,0:T(8,128)} %bitcast.5), channel_id=1, replica_groups=mesh['ent'=64,'rep'=4] {'rep'}, dimensions={0}, use_global_device_ids=true | all-gather | bytes 1054720 | tf_op jit(solution)/shard_map/all_gather | solution.py:37
  28.1 0.1 reshape.46
  28.2 1.6 gather_fusion.1
  29.8 0.1 broadcast_select_fusion.1
  30.0 1.6 gather_fusion.2
  31.5 0.1 broadcast_select_fusion
  31.7 165.3 %all-reduce.3.cloned.1.call-done = f32[512,256]{1,0:T(8,128)} async-done(((f32[512,256]{1,0:T(8,128)}), f32[512,256]{1,0:T(8,128)}) %all-reduce.3.cloned.1.call-update) | async-done | bytes 524304 | tf_op jit(solution)/shard_map/psum | solution.py:36
  197.0 1.1 multiply_subtract_fusion.1
  198.1 10.9 %fusion.13 = (f32[512]{0:T(512)S(1)}, f32[512,4096]{1,0:T(8,128)}) fusion(f32[4096,256]{1,0:T(8,128)} %param.7, f32[512,128]{1,0:T(8,128)S(1)} %get-tuple-element.11, f32[512,128]{1,0:T(8,128)S(1)} %get-tuple-element.10), kind=kOutput, calls=%fused_computation.37 | convolution fusion | flops 6444678656 | bytes 13109248 | tf_op jit(solution)/shard_map/dot_general | solution.py:15
  209.0 126.3 %pmax.14 = f32[512]{0:T(512)S(1)} all-reduce(f32[512]{0:T(512)S(1)} %get-tuple-element.13), channel_id=1, replica_groups=mesh['ent'=64,'rep'=4] {'ent'}, use_global_device_ids=true, to_apply=%region_2.4 | all-reduce | flops 512 | bytes 4096 | tf_op jit(solution)/shard_map/pmax | solution.py:43
  335.3 11.2 %fusion.1 = f32[512,256]{1,0:T(8,128)} fusion(f32[4096,256]{1,0:T(8,128)} %param.7, f32[512,4096]{1,0:T(8,128)} %get-tuple-element.14, f32[512]{0:T(512)S(1)} %pmax.14), kind=kOutput, calls=%fused_computation.7 | convolution fusion | flops 6444548096 | bytes 13109248 | tf_op jit(solution)/shard_map/dot_general | solution.py:25
  346.5 0.0 all-reduce.5.cloned.1.call-update
  346.5 4.6 fusion
  351.1 125.4 %psum.23 = f32[512]{0:T(512)S(1)} all-reduce(f32[512]{0:T(512)S(1)} %fusion), channel_id=1, replica_groups=mesh['ent'=64,'rep'=4] {'ent'}, use_global_device_ids=true, to_apply=%region_5.7 | all-reduce | flops 512 | bytes 4096 | tf_op jit(solution)/shard_map/psum | solution.py:45
  476.5 50.5 %all-reduce.5.cloned.1.call-done = f32[512,256]{1,0:T(8,128)} async-done(((f32[512,256]{1,0:T(8,128)}), f32[512,256]{1,0:T(8,128)}) %all-reduce.5.cloned.1.call-update) | async-done | bytes 524304 | tf_op jit(solution)/shard_map/psum | solution.py:45
  527.0 1.2 broadcast_divide_fusion
  528.2 0.1 multiply_subtract_fusion
  528.3 10.9 %fusion.14 = (f32[512]{0:T(512)S(1)}, f32[512,4096]{1,0:T(8,128)}) fusion(f32[4096,256]{1,0:T(8,128)} %param.7, f32[512,128]{1,0:T(8,128)S(1)} %get-tuple-element.9, f32[512,128]{1,0:T(8,128)S(1)} %get-tuple-element.8), kind=kOutput, calls=%fused_computation.38 | convolution fusion | flops 6444678656 | bytes 13109248 | tf_op jit(solution)/shard_map/dot_general | solution.py:15
  539.2 126.3 %pmax.15 = f32[512]{0:T(512)S(1)} all-reduce(f32[512]{0:T(512)S(1)} %get-tuple-element.15), channel_id=1, replica_groups=mesh['ent'=64,'rep'=4] {'ent'}, use_global_device_ids=true, to_apply=%region_7.9 | all-reduce | flops 512 | bytes 4096 | tf_op jit(solution)/shard_map/pmax | solution.py:49
  665.5 4.6 exponential_reduce_fusion
  670.1 48.2 %all-gather.2 = f32[64,1,512]{2,1,0:T(1,128)S(1)} all-gather(f32[1,1,512]{2,1,0:T(1,128)S(1)} %bitcast.6), channel_id=2, replica_groups=mesh['ent'=64,'rep'=4] {'ent'}, dimensions={0}, use_global_device_ids=true | all-gather | bytes 133120 | tf_op jit(solution)/shard_map/all_gather | solution.py:51
  718.3 0.1 reduce_sum.29
  718.4 8.6 %subtract_subtract_fusion = f32[512,4096]{1,0:T(8,128)} fusion(f32[512,4096]{1,0:T(8,128)} %get-tuple-element.16, f32[512]{0:T(512)S(1)} %log.7, f32[512]{0:T(512)S(1)} %pmax.15), kind=kLoop, calls=%fused_computation.5 | loop fusion | flops 4194304 | bytes 16781312 | tf_op jit(solution)/shard_map/sub | solution.py:52
  (4 shorter events, 0.0 us)
Async XLA Ops:
  6.5 190.5 %all-reduce.3.cloned.1.call-start = ((), (), s32[]{:S(2)}) async-start(), calls=%async_computation | async-start | bytes 1048576 | tf_op jit(solution)/shard_map/psum | solution.py:36
  12.0 515.0 %all-reduce.5.cloned.1.call-start = ((), (), s32[]{:S(2)}) async-start(), calls=%async_computation.1 | async-start | bytes 1048576 | tf_op jit(solution)/shard_map/psum | solution.py:45
Sparse Core Ops, SparseCore 0:
  12.1 184.8 all-reduce.2
  346.6 180.3 all-reduce.4
